TPU v7x, 512 devices: a whole 4x4x16 slice. The times are simulated.
512 devices in a mesh: rep: 8 (over y, core), expert: 64 (over x, z).
Axes of the slice: x: 4, y: 4, z: 16, core: 2. Of those that a mesh axis runs over, the one named last changes fastest.
Arguments:
- tokens: bfloat16 [8192, 4096], P('expert', 'rep')
- norm_gain: float32 [4096], P('rep'), may hold values from 0.25 to 1.75
- gate_weights: float32 [8192, 8], P('expert'), may hold values from 0.1 to 0.6
- exit_flags: int32 [8192], P('expert'), may hold values from 0 to 1, as said below
- routes: int32 [8192, 8], P('expert'), may hold values from 0 to 127, as said below
- next_device: int32 [8192], P('expert'), may hold values from 0 to 63, as said below
- up_weight: bfloat16 [128, 4096, 1024], P('expert', 'rep'), may hold values from -0.09375 to 0.09375
- down_weight: bfloat16 [128, 1024, 4096], P('expert', None, 'rep'), may hold values from -0.1875 to 0.1875
Outputs:
- handed: float32 [4096, 4096], P('expert', 'rep')
Inputs may be any that keep to these rules, and one draw needn't show every extreme that they name: `exit_flags`: one block of 128 rows holds at most 64 live rows; some block holds exactly 64. `routes`: each row names 8 different experts. Among the live rows of one block, every expert is named the same number of times up to one, so at most 4 times; a block with 64 live rows names every expert exactly 4 times. `next_device`: among the live rows of one block, every value is named the same number of times up to one, so at most 1 times.
All inputs are finite; a program needn't handle non-finite values.
Results may differ from a plain program's by a relative error of at most 0.0017.
Values may be sent and summed in bfloat16 or wider, within the bound.
No kernel may reach another device: no remote copies, remote signals or barrier semaphores. Data moves between devices by JAX's collectives and lax.ppermute only.
A program may use at most 64 MiB of HBM per device.

v0:
```python
import jax
import jax.numpy as jnp
from jax import lax
from jax.sharding import PartitionSpec as P


def per_device(
    tokens, norm_gain, gate_weights, exit_flags, routes, next_device, up_weight, down_weight
):
    row_count, feat_width = tokens.shape
    owner_count = lax.axis_size("expert")
    rep_count = lax.axis_size("rep")
    local_experts = up_weight.shape[0]
    route_count = routes.shape[1]
    experts_all = local_experts * owner_count
    most_live = row_count // 2
    capacity = route_count * most_live // experts_all
    hand_cap = (most_live + owner_count - 1) // owner_count
    slot_total = local_experts * owner_count * capacity
    widened = tokens.astype(jnp.float32)
    squares = lax.psum(jnp.sum(widened * widened, axis=1), "rep")
    rinv_rows = lax.rsqrt(squares / (feat_width * rep_count) + 1e-06)
    normed = (widened * rinv_rows[:, None] * norm_gain[None, :]).astype(jnp.bfloat16)
    survive = 1 - exit_flags
    pair_live = jnp.repeat(survive, route_count)
    route_flat = routes.reshape(-1)
    one_hot = (route_flat[:, None] == jnp.arange(experts_all, dtype=jnp.int32)[None, :]).astype(
        jnp.int32
    ) * pair_live[:, None]
    earlier = jnp.cumsum(one_hot, axis=0) - one_hot
    position = jnp.sum(earlier * one_hot, axis=1)
    owner_id = route_flat // local_experts
    local_id = route_flat % local_experts
    slot_index = (local_id * owner_count + owner_id) * capacity + position
    slot_index = jnp.where(pair_live > 0, slot_index, slot_total)
    pair_row = jnp.arange(row_count * route_count, dtype=jnp.int32) // route_count
    source_row = jnp.zeros((slot_total,), jnp.int32).at[slot_index].set(pair_row + 1, mode="drop")
    padded = jnp.concatenate([jnp.zeros((1, feat_width), jnp.bfloat16), normed], axis=0)
    outbound = padded[source_row].reshape(local_experts, owner_count, capacity, feat_width)
    received = lax.all_to_all(outbound, "expert", split_axis=1, concat_axis=1, tiled=True)
    item_count = received.shape[2]
    flattened = received.reshape(local_experts, owner_count * item_count, feat_width)
    partial_value = jnp.einsum(
        "erd,edh->erh", flattened, up_weight, preferred_element_type=jnp.float32
    )
    summed = lax.psum(partial_value, "rep")
    activated = jax.nn.silu(summed).astype(jnp.bfloat16)
    expert_out = jnp.einsum(
        "erh,ehd->erd", activated, down_weight, preferred_element_type=jnp.float32
    )
    expert_out = expert_out.astype(jnp.bfloat16).reshape(
        local_experts, owner_count, item_count, feat_width
    )
    returned = lax.all_to_all(expert_out, "expert", split_axis=1, concat_axis=1, tiled=True)
    flat_back = returned.reshape(slot_total, feat_width)
    picked = flat_back[jnp.minimum(slot_index, slot_total - 1)].reshape(
        row_count, route_count, feat_width
    )
    mixture = jnp.einsum("rk,rkd->rd", gate_weights, picked, preferred_element_type=jnp.float32)
    updated = widened + mixture
    dest_hot = (next_device[:, None] == jnp.arange(owner_count, dtype=jnp.int32)[None, :]).astype(
        jnp.int32
    ) * survive[:, None]
    dest_before = jnp.cumsum(dest_hot, axis=0) - dest_hot
    handoff_pos = jnp.sum(dest_before * dest_hot, axis=1)
    hand_slot = jnp.where(survive > 0, next_device * hand_cap + handoff_pos, owner_count * hand_cap)
    row_plus = jnp.arange(row_count, dtype=jnp.int32) + 1
    target = (
        jnp.zeros((owner_count * hand_cap,), jnp.int32).at[hand_slot].set(row_plus, mode="drop")
    )
    stacked = jnp.concatenate([jnp.zeros((1, feat_width), jnp.float32), updated], axis=0)
    leaving = stacked[target].reshape(owner_count, hand_cap, feat_width)
    arrived = lax.all_to_all(leaving, "expert", split_axis=0, concat_axis=0, tiled=True)
    return arrived.reshape(owner_count * hand_cap, feat_width)


def solution(mesh):
    in_specs = (
        P("expert", "rep"),
        P("rep"),
        P("expert", None),
        P("expert"),
        P("expert", None),
        P("expert"),
        P("expert", "rep", None),
        P("expert", None, "rep"),
    )
    out_specs = P("expert", "rep")
    return jax.shard_map(
        per_device, mesh=mesh, in_specs=in_specs, out_specs=out_specs, check_vma=False
    )
```

profile of v0, /device:TPU:24, one launch (start us, length us, event | category | flops | bytes accessed | tf_op | source)
XLA Modules:
  0.0 243.5 jit_solution(2612807899074196465)
XLA Ops:
  6.5 0.9 copy.16
  7.5 0.1 eq.40
  7.6 0.1 eq.44
  7.7 0.1 reshape.226
  7.8 0.7 broadcast_subtract_fusion
  8.4 0.7 broadcast_compare_fusion
  9.1 0.1 broadcast_in_dim.39
  9.2 0.1 copy.19
  9.3 0.1 copy.18
  9.4 0.3 fusion.3
  9.8 0.1 copy.20
  9.9 0.1 broadcast_in_dim.42
  10.0 0.1 mul.96
  10.1 0.1 broadcast_in_dim.38
  10.2 0.1 gt.20
  10.3 0.5 fusion.2
  10.8 4.3 %scatter_custom_fusion = s32[512]{0:T(512)S(1)} fusion(s32[1024]{0:T(1024)S(1)} %bitcast.29, s32[1024]{0:T(1024)S(1)} %fusion.13, s32[]{:T(128)} %constant.69.clone.1), kind=kCustom, calls=%fused_computation.56 | custom fusion | bytes 2052 | tf_op jit(solution)/shard_map/scatter | solution.py:37
  15.2 0.1 fusion.5
  15.3 14.0 %psum.14 = f32[128]{0:T(128)S(1)} all-reduce(f32[128]{0:T(128)S(1)} %fusion.5), channel_id=1, replica_groups=mesh['rep'=8,'expert'=64] {'rep'}, use_global_device_ids=true, to_apply=%region_1.0 | all-reduce | flops 128 | bytes 1024 | tf_op jit(solution)/shard_map/psum | solution.py:21
  29.4 0.1 fusion.7
  29.5 2.0 gather_fusion
  31.5 0.1 reshape.228
  31.6 0.2 copy.22
  31.8 46.3 %all_to_all.15 = bf16[2,64,4,512]{3,2,0,1:T(4,128)(2,1)S(1)} all-to-all(bf16[2,64,4,512]{3,2,0,1:T(4,128)(2,1)S(1)} %copy.22), channel_id=1, replica_groups=mesh['rep'=8,'expert'=64] {'expert'}, dimensions={1} | all-to-all | bytes 1048576 | tf_op jit(solution)/shard_map/all_to_all | solution.py:40
  78.1 0.2 copy.23
  78.3 0.1 reshape.229
  78.4 2.0 fusion.25
  80.5 0.0 all-reduce.4.cloned.1.call-update
  80.5 72.3 %all-reduce.4.cloned.1.call-done = f32[2,256,1024]{2,1,0:T(8,128)} async-done(((f32[2,256,1024]{2,1,0:T(8,128)}), f32[2,256,1024]{2,1,0:T(8,128)}) %all-reduce.4.cloned.1.call-update) | async-done | bytes 2097168 | tf_op jit(solution)/shard_map/psum | solution.py:46
  152.8 3.0 %convolution_convert_fusion = bf16[2,256,512]{2,1,0:T(8,128)(2,1)S(1)} fusion(bf16[2,1024,512]{2,1,0:T(8,128)(2,1)} %param.15, f32[2,256,1024]{2,1,0:T(8,128)} %all-reduce.4.cloned.1.call-done), kind=kOutput, calls=%fused_computation.6 | convolution fusion | flops 539754496 | bytes 4718592 | tf_op jit(solution)/shard_map/erh,ehd->erd/dot_general | solution.py:48
  155.8 0.0 copy-start.2
  155.8 0.1 reshape.230
  155.9 1.0 copy.24
  156.9 15.6 %all-to-all-start.1 = ((bf16[2,64,4,512]{3,2,0,1:T(4,128)(2,1)}), bf16[2,64,4,512]{3,2,0,1:T(4,128)(2,1)S(1)}, u32[]{:S(2)}, u32[]{:S(2)}) async-start(bf16[2,64,4,512]{3,2,0,1:T(4,128)(2,1)} %copy.24), calls=%async_computation.1 | async-start | bytes 1048576 | tf_op jit(solution)/shard_map/all_to_all | solution.py:54
  172.5 0.1 copy.27
  172.7 0.1 fusion.12
  172.8 0.2 reduce_window_sum.28
  173.0 0.2 fusion.11
  173.2 1.0 scatter_custom_fusion.1
  174.2 29.5 %all-to-all-done.1 = bf16[2,64,4,512]{3,2,0,1:T(4,128)(2,1)S(1)} async-done(((bf16[2,64,4,512]{3,2,0,1:T(4,128)(2,1)}), bf16[2,64,4,512]{3,2,0,1:T(4,128)(2,1)S(1)}, u32[]{:S(2)}, u32[]{:S(2)}) %all-to-all-start.1) | async-done | bytes 524320 | tf_op jit(solution)/shard_map/all_to_all | solution.py:54
  203.7 0.2 copy.25
  203.8 0.1 reshape.231
  204.0 5.1 %gather_fusion.1 = bf16[1024,512]{1,0:T(8,128)(2,1)} fusion(bf16[512,512]{1,0:T(8,128)(2,1)S(1)} %reshape.231, s32[1024]{0:T(1024)S(1)} %broadcast_clamp_fusion), kind=kCustom, calls=%fused_computation.1 | custom fusion | bytes 2101248 | tf_op jit(solution)/shard_map/gather | solution.py:56
  209.0 1.6 fusion
  210.8 0.7 gather_fusion.2
  211.4 0.1 copy.26
  211.6 24.5 %all_to_all.16 = f32[64,1,512]{2,1,0:T(1,128)S(1)} all-to-all(f32[64,1,512]{2,1,0:T(1,128)S(1)} %copy.26), channel_id=1, replica_groups=mesh['rep'=8,'expert'=64] {'expert'}, dimensions={0} | all-to-all | bytes 262144 | tf_op jit(solution)/shard_map/all_to_all | solution.py:73
  236.0 0.7 copy.32
  (30 shorter events, 0.3 us)
Async XLA Ops:
  6.5 71.9 %copy-start = (bf16[2,512,1024]{2,1,0:T(8,128)(2,1)S(1)}, bf16[2,512,1024]{2,1,0:T(8,128)(2,1)}, u32[]{:S(2)}) copy-start(bf16[2,512,1024]{2,1,0:T(8,128)(2,1)} %param.14) | copy-start | bytes 6291460
  6.5 8.6 %copy-start.1 = (bf16[128,512]{1,0:T(8,128)(2,1)S(1)}, bf16[128,512]{1,0:T(8,128)(2,1)}, u32[]{:S(2)}) copy-start(bf16[128,512]{1,0:T(8,128)(2,1)} %param.8) | copy-start | bytes 393220
  6.5 22.8 %copy-start.4 = (f32[512]{0:T(512)S(1)}, f32[512]{0:T(512)}, u32[]{:S(2)}) copy-start(f32[512]{0:T(512)} %param.9) | copy-start | bytes 6148
  6.5 146.2 %all-reduce.4.cloned.1.call-start = ((), (), s32[]{:S(2)}) async-start(), calls=%async_computation.3 | async-start | bytes 4194304 | tf_op jit(solution)/shard_map/psum | solution.py:46
  155.8 16.8 %copy-start.3 = (f32[128,8]{0,1:T(8,128)S(1)}, f32[128,8]{0,1:T(8,128)}, u32[]{:S(2)}) copy-start(f32[128,8]{0,1:T(8,128)} %param.10) | copy-start | bytes 12292
  155.8 16.9 %copy-start.2 = (s32[128]{0:T(128)S(1)}, s32[128]{0:T(128)}, u32[]{:S(2)}) copy-start(s32[128]{0:T(128)} %param.13) | copy-start | bytes 1540
  155.8 17.4 %copy-start.5 = (s32[128]{0:T(128)S(1)}, s32[128]{0:T(128)}, u32[]{:S(2)}) copy-start(s32[128]{0:T(128)} %param.11) | copy-start | bytes 1540
  156.9 46.8 %all-to-all-start.1 = ((bf16[2,64,4,512]{3,2,0,1:T(4,128)(2,1)}), bf16[2,64,4,512]{3,2,0,1:T(4,128)(2,1)S(1)}, u32[]{:S(2)}, u32[]{:S(2)}) async-start(bf16[2,64,4,512]{3,2,0,1:T(4,128)(2,1)} %copy.24), calls=%async_computation.1 | async-start | bytes 1048576 | tf_op jit(solution)/shard_map/all_to_all | solution.py:54
Sparse Core Ops, SparseCore 0:
  80.6 72.1 all-reduce.3
where the time goes:
time: 244 us
  waiting for transfers between devices  102 us (42%)
  blocking collectives  84.8 us (35%)
  local copies, waits for them, and re-layouts  18 us (7%)
  starting transfers between devices  15.6 us (6%)
  between operations  13.7 us (6%)
  matrix products  6.6 us (3%)
  other arithmetic  3.01 us (1%)
    psum x1, waiting for transfers between devices, per_device(): summed = lax.psum(partial_value, 'rep')  72.3 us
    all_to_all x1, blocking collectives, per_device(): lax.all_to_all(outbound, 'expert', split_axis=1, concat_axis=1, tiled=True)  46.3 us
    all_to_all x1, waiting for transfers between devices, per_device(): lax.all_to_all(expert_out, 'expert', split_axis=1, concat_axis=1, tiled=T...  29.5 us
    all_to_all x1, blocking collectives, per_device(): lax.all_to_all(leaving, 'expert', split_axis=0, concat_axis=0, tiled=True)  24.5 us
    all_to_all x1, starting transfers between devices, per_device(): lax.all_to_all(expert_out, 'expert', split_axis=1, concat_axis=1, tiled=T...  15.6 us
    psum x1, blocking collectives, per_device(): squares = lax.psum(jnp.sum(widened * widened, axis=1), 'rep')  14 us
    gather x1, local copies, waits for them, and re-layouts, per_device(): flat_back[jnp.minimum(slot_index, slot_total - 1)]  5.07 us
  transfers between devices with their start and end apart: 2, of which 2 were waited for; matrix products, arithmetic and copies ran while one was open for 1% of the time, Pallas kernels for 0%

commit v1 on v0

--- a/solution.py
+++ b/solution.py
@@ -2,6 +2,25 @@
 import jax.numpy as jnp
 from jax import lax
 from jax.sharding import PartitionSpec as P
+
+
+def show_the_flows(local_block, which_axis):
+    world_n = lax.axis_size(which_axis)
+
+    def post_turns(left_arr, parts_out):
+        if parts_out >= world_n:
+            return left_arr
+        y1 = post_turns(
+            left_arr
+            + lax.ppermute(
+                left_arr, axis_name=which_axis, perm=[(q, q ^ parts_out) for q in range(world_n)]
+            ),
+            2 * parts_out,
+        )
+        return y1
+
+    part_now = post_turns(local_block, 1)
+    return part_now
 
 
 def per_device(
@@ -43,7 +62,7 @@
     partial_value = jnp.einsum(
         "erd,edh->erh", flattened, up_weight, preferred_element_type=jnp.float32
     )
-    summed = lax.psum(partial_value, "rep")
+    summed = show_the_flows(partial_value, "rep")
     activated = jax.nn.silu(summed).astype(jnp.bfloat16)
     expert_out = jnp.einsum(
         "erh,ehd->erd", activated, down_weight, preferred_element_type=jnp.float32

time: 244 us -> 252 us (1.033)
  waiting for transfers between devices: 102 us -> 127 us
  between operations: 13.7 us -> 0.39 us
  matrix products: 6.6 us -> 3.08 us
    ppermute x0 -> x3, waiting for transfers between devices: none -> 99.3 us  [post_turns(): lax.ppermute(left_arr, axis_name=which_axis, perm=[(q, q ^ parts_out) for...]
    psum x1 -> x0, waiting for transfers between devices: 72.3 us -> none  [per_device(): summed = lax.psum(partial_value, 'rep')]
    all_to_all x1, starting transfers between devices: 15.6 us -> 6.74 us  [per_device(): lax.all_to_all(expert_out, 'expert', split_axis=1, concat_axis=1, tiled=T...]
    ppermute x0 -> x3, starting transfers between devices: none -> 7.95 us  [post_turns(): lax.ppermute(left_arr, axis_name=which_axis, perm=[(q, q ^ parts_out) for...]
  transfers between devices with their start and end apart: 2 -> 4, of which waited for: 2 -> 4; matrix products, arithmetic and copies ran while one was open for 1% -> 1% of each run, Pallas kernels for 0% -> 0%
where the time goes in v1:
time: 252 us; the launch traced here: 251 us
  waiting for transfers between devices  127 us (50%)
  blocking collectives  82.9 us (33%)
  local copies, waits for them, and re-layouts  18 us (7%)
  starting transfers between devices  14.7 us (6%)
  other arithmetic  4.11 us (2%)
  matrix products  3.08 us (1%)
    ppermute x3, waiting for transfers between devices, post_turns(): lax.ppermute(left_arr, axis_name=which_axis, perm=[(q, q ^ parts_out) for...  99.3 us
    all_to_all x1, blocking collectives, per_device(): lax.all_to_all(outbound, 'expert', split_axis=1, concat_axis=1, tiled=True)  46.3 us
    all_to_all x1, waiting for transfers between devices, per_device(): lax.all_to_all(expert_out, 'expert', split_axis=1, concat_axis=1, tiled=T...  28.2 us
    all_to_all x1, blocking collectives, per_device(): lax.all_to_all(leaving, 'expert', split_axis=0, concat_axis=0, tiled=True)  22.5 us
    psum x1, blocking collectives, per_device(): squares = lax.psum(jnp.sum(widened * widened, axis=1), 'rep')  14 us
    ppermute x3, starting transfers between devices, post_turns(): lax.ppermute(left_arr, axis_name=which_axis, perm=[(q, q ^ parts_out) for...  7.95 us
    all_to_all x1, starting transfers between devices, per_device(): lax.all_to_all(expert_out, 'expert', split_axis=1, concat_axis=1, tiled=T...  6.74 us
    gather x1, local copies, waits for them, and re-layouts, per_device(): flat_back[jnp.minimum(slot_index, slot_total - 1)]  5.07 us
  transfers between devices with their start and end apart: 4, of which 4 were waited for; matrix products, arithmetic and copies ran while one was open for 1% of the time, Pallas kernels for 0%

profile of v1, /device:TPU:24, one launch (start us, length us, event | category | flops | bytes accessed | tf_op | source)
XLA Modules:
  0.0 250.6 jit_solution(6085079943754631807)
XLA Ops:
  0.0 0.9 copy.16
  0.9 0.1 eq.40
  1.1 0.1 reshape.226
  1.2 0.7 broadcast_subtract_fusion
  1.9 0.7 broadcast_compare_fusion
  2.7 0.1 copy.18
  2.8 0.3 fusion.3
  3.2 0.1 copy.20
  3.4 0.1 mul.96
  3.6 0.1 gt.20
  3.7 0.5 fusion.2
  4.3 4.3 %scatter_custom_fusion = s32[512]{0:T(512)S(1)} fusion(s32[1024]{0:T(1024)S(1)} %bitcast.29, s32[1024]{0:T(1024)S(1)} %fusion.13, s32[]{:T(128)} %constant.69.clone.1), kind=kCustom, calls=%fused_computation.56 | custom fusion | bytes 2052 | tf_op jit(solution)/shard_map/scatter | solution.py:56
  8.6 0.1 fusion.5
  8.8 14.0 %psum.7 = f32[128]{0:T(128)S(1)} all-reduce(f32[128]{0:T(128)S(1)} %fusion.5), channel_id=1, replica_groups=mesh['rep'=8,'expert'=64] {'rep'}, use_global_device_ids=true, to_apply=%region_1.0 | all-reduce | flops 128 | bytes 1024 | tf_op jit(solution)/shard_map/psum | solution.py:40
  22.8 0.1 fusion.7
  23.0 2.0 gather_fusion
  24.9 0.1 reshape.228
  25.1 0.2 copy.22
  25.3 46.3 %all_to_all.15 = bf16[2,64,4,512]{3,2,0,1:T(4,128)(2,1)S(1)} all-to-all(bf16[2,64,4,512]{3,2,0,1:T(4,128)(2,1)S(1)} %copy.22), channel_id=1, replica_groups=mesh['rep'=8,'expert'=64] {'expert'}, dimensions={1} | all-to-all | bytes 1048576 | tf_op jit(solution)/shard_map/all_to_all | solution.py:59
  71.6 0.2 copy.23
  71.8 0.1 reshape.229
  71.9 0.7 fusion.25
  72.6 3.1 %collective-permute-start = (f32[2,256,1024]{2,1,0:T(8,128)S(1)}, f32[2,256,1024]{2,1,0:T(8,128)S(1)}, u32[]{:S(2)}, u32[]{:S(2)}) collective-permute-start(f32[2,256,1024]{2,1,0:T(8,128)S(1)} %fusion.25), channel_id=1, source_target_pairs={{0,64},{64,0},{128,192},{192,128},{256,320},{320,256},{384,448},{4... | collective-permute-start | bytes 6291464 | tf_op jit(solution)/shard_map/ppermute | solution.py:15
  75.7 3.8 %collective-permute-done = f32[2,256,1024]{2,1,0:T(8,128)S(1)} collective-permute-done((f32[2,256,1024]{2,1,0:T(8,128)S(1)}, f32[2,256,1024]{2,1,0:T(8,128)S(1)}, u32[]{:S(2)}, u32[]{:S(2)}) %collective-permute-start) | collective-permute-done | bytes 2097184 | tf_op jit(solution)/shard_map/ppermute | solution.py:15
  79.5 0.5 add.141
  80.1 2.1 collective-permute-start.1
  82.1 47.9 %collective-permute-done.1 = f32[2,256,1024]{2,1,0:T(8,128)S(1)} collective-permute-done((f32[2,256,1024]{2,1,0:T(8,128)S(1)}, f32[2,256,1024]{2,1,0:T(8,128)S(1)}, u32[]{:S(2)}, u32[]{:S(2)}) %collective-permute-start.1) | collective-permute-done | bytes 2097184 | tf_op jit(solution)/shard_map/ppermute | solution.py:15
  130.0 0.6 add.142
  130.6 2.8 %collective-permute-start.2 = (f32[2,256,1024]{2,1,0:T(8,128)S(1)}, f32[2,256,1024]{2,1,0:T(8,128)S(1)}, u32[]{:S(2)}, u32[]{:S(2)}) collective-permute-start(f32[2,256,1024]{2,1,0:T(8,128)S(1)} %add.142), channel_id=1, source_target_pairs={{0,256},{64,320},{128,384},{192,448},{256,0},{320,64},{384,128},{4... | collective-permute-start | bytes 6291464 | tf_op jit(solution)/shard_map/ppermute | solution.py:15
  133.4 47.7 %collective-permute-done.2 = f32[2,256,1024]{2,1,0:T(8,128)S(1)} collective-permute-done((f32[2,256,1024]{2,1,0:T(8,128)S(1)}, f32[2,256,1024]{2,1,0:T(8,128)S(1)}, u32[]{:S(2)}, u32[]{:S(2)}) %collective-permute-start.2) | collective-permute-done | bytes 2097184 | tf_op jit(solution)/shard_map/ppermute | solution.py:15
  181.0 0.7 convolution_convert_fusion
  181.8 0.1 reshape.230
  181.9 1.0 copy.24
  182.9 6.7 %all-to-all-start.1 = ((bf16[2,64,4,512]{3,2,0,1:T(4,128)(2,1)}), bf16[2,64,4,512]{3,2,0,1:T(4,128)(2,1)S(1)}, u32[]{:S(2)}, u32[]{:S(2)}) async-start(bf16[2,64,4,512]{3,2,0,1:T(4,128)(2,1)} %copy.24), calls=%async_computation.1 | async-start | bytes 1048576 | tf_op jit(solution)/shard_map/all_to_all | solution.py:73
  189.6 0.1 copy.27
  189.8 0.1 fusion.12
  189.9 0.2 reduce_window_sum.28
  190.1 0.2 fusion.11
  190.3 1.0 scatter_custom_fusion.1
  191.3 28.2 %all-to-all-done.1 = bf16[2,64,4,512]{3,2,0,1:T(4,128)(2,1)S(1)} async-done(((bf16[2,64,4,512]{3,2,0,1:T(4,128)(2,1)}), bf16[2,64,4,512]{3,2,0,1:T(4,128)(2,1)S(1)}, u32[]{:S(2)}, u32[]{:S(2)}) %all-to-all-start.1) | async-done | bytes 524320 | tf_op jit(solution)/shard_map/all_to_all | solution.py:73
  219.5 0.2 copy.25
  219.7 0.1 reshape.231
  219.8 5.1 %gather_fusion.1 = bf16[1024,512]{1,0:T(8,128)(2,1)} fusion(bf16[512,512]{1,0:T(8,128)(2,1)S(1)} %reshape.231, s32[1024]{0:T(1024)S(1)} %broadcast_clamp_fusion), kind=kCustom, calls=%fused_computation.1 | custom fusion | bytes 2101248 | tf_op jit(solution)/shard_map/gather | solution.py:75
  224.9 1.6 fusion
  226.6 0.7 gather_fusion.2
  227.2 0.1 copy.26
  227.4 22.5 %all_to_all.16 = f32[64,1,512]{2,1,0:T(1,128)S(1)} all-to-all(f32[64,1,512]{2,1,0:T(1,128)S(1)} %copy.26), channel_id=1, replica_groups=mesh['rep'=8,'expert'=64] {'expert'}, dimensions={0} | all-to-all | bytes 262144 | tf_op jit(solution)/shard_map/all_to_all | solution.py:92
  249.9 0.7 copy.32
  (37 shorter events, 0.7 us)
Async XLA Ops:
  0.0 71.9 %copy-start = (bf16[2,512,1024]{2,1,0:T(8,128)(2,1)S(1)}, bf16[2,512,1024]{2,1,0:T(8,128)(2,1)}, u32[]{:S(2)}) copy-start(bf16[2,512,1024]{2,1,0:T(8,128)(2,1)} %param.14) | copy-start | bytes 6291460
  0.0 8.6 %copy-start.1 = (bf16[128,512]{1,0:T(8,128)(2,1)S(1)}, bf16[128,512]{1,0:T(8,128)(2,1)}, u32[]{:S(2)}) copy-start(bf16[128,512]{1,0:T(8,128)(2,1)} %param.8) | copy-start | bytes 393220
  0.0 22.8 %copy-start.4 = (f32[512]{0:T(512)S(1)}, f32[512]{0:T(512)}, u32[]{:S(2)}) copy-start(f32[512]{0:T(512)} %param.9) | copy-start | bytes 6148
  72.6 6.9 %collective-permute-start = (f32[2,256,1024]{2,1,0:T(8,128)S(1)}, f32[2,256,1024]{2,1,0:T(8,128)S(1)}, u32[]{:S(2)}, u32[]{:S(2)}) collective-permute-start(f32[2,256,1024]{2,1,0:T(8,128)S(1)} %fusion.25), channel_id=1, source_target_pairs={{0,64},{64,0},{128,192},{192,128},{256,320},{320,256},{384,448},{4... | collective-permute-start | bytes 6291464 | tf_op jit(solution)/shard_map/ppermute | solution.py:15
  80.1 101.0 %copy-start.6 = (bf16[2,1024,512]{2,1,0:T(8,128)(2,1)S(1)}, bf16[2,1024,512]{2,1,0:T(8,128)(2,1)}, u32[]{:S(2)}) copy-start(bf16[2,1024,512]{2,1,0:T(8,128)(2,1)} %param.15) | copy-start | bytes 6291460
  80.1 49.9 %collective-permute-start.1 = (f32[2,256,1024]{2,1,0:T(8,128)S(1)}, f32[2,256,1024]{2,1,0:T(8,128)S(1)}, u32[]{:S(2)}, u32[]{:S(2)}) collective-permute-start(f32[2,256,1024]{2,1,0:T(8,128)S(1)} %add.141), channel_id=1, source_target_pairs={{0,128},{64,192},{128,0},{192,64},{256,384},{320,448},{384,256},{4... | collective-permute-start | bytes 6291464 | tf_op jit(solution)/shard_map/ppermute | solution.py:15
  130.6 50.5 %collective-permute-start.2 = (f32[2,256,1024]{2,1,0:T(8,128)S(1)}, f32[2,256,1024]{2,1,0:T(8,128)S(1)}, u32[]{:S(2)}, u32[]{:S(2)}) collective-permute-start(f32[2,256,1024]{2,1,0:T(8,128)S(1)} %add.142), channel_id=1, source_target_pairs={{0,256},{64,320},{128,384},{192,448},{256,0},{320,64},{384,128},{4... | collective-permute-start | bytes 6291464 | tf_op jit(solution)/shard_map/ppermute | solution.py:15
  181.8 7.9 %copy-start.3 = (f32[128,8]{0,1:T(8,128)S(1)}, f32[128,8]{0,1:T(8,128)}, u32[]{:S(2)}) copy-start(f32[128,8]{0,1:T(8,128)} %param.10) | copy-start | bytes 12292
  181.8 8.0 %copy-start.2 = (s32[128]{0:T(128)S(1)}, s32[128]{0:T(128)}, u32[]{:S(2)}) copy-start(s32[128]{0:T(128)} %param.13) | copy-start | bytes 1540
  181.8 8.5 %copy-start.5 = (s32[128]{0:T(128)S(1)}, s32[128]{0:T(128)}, u32[]{:S(2)}) copy-start(s32[128]{0:T(128)} %param.11) | copy-start | bytes 1540
  182.9 36.6 %all-to-all-start.1 = ((bf16[2,64,4,512]{3,2,0,1:T(4,128)(2,1)}), bf16[2,64,4,512]{3,2,0,1:T(4,128)(2,1)S(1)}, u32[]{:S(2)}, u32[]{:S(2)}) async-start(bf16[2,64,4,512]{3,2,0,1:T(4,128)(2,1)} %copy.24), calls=%async_computation.1 | async-start | bytes 1048576 | tf_op jit(solution)/shard_map/all_to_all | solution.py:73
